TPU v7x, 128 devices: a whole 4x4x4 slice. The times are simulated.
128 devices in a mesh: ctx: 16 (over z, x_lo, core), head: 8 (over y, x_hi).
Axes of the slice: x: 4 (x_hi: 2, x_lo: 2; x = x_hi * 2 + x_lo), y: 4, z: 4, core: 2. Of those that a mesh axis runs over, the one named last changes fastest.
Arguments:
- queries: bfloat16 [24576, 3072], P('ctx', 'head'), may hold values from -160 to 160
- key_states: bfloat16 [24576, 3072], P('ctx', 'head'), may hold values from -12 to 12
- value_states: bfloat16 [24576, 3072], P('ctx', 'head'), may hold values from -18 to 18
- out_grads: bfloat16 [24576, 3072], P(('ctx', 'head')), may hold values from -6 to 6
- pattern: int32 [64, 8], replicated, may hold values from -1 to 63, as said below
Outputs:
- attended: bfloat16 [24576, 3072], P(('ctx', 'head'))
- query_grads: bfloat16 [24576, 3072], P('ctx', 'head')
- key_grads: bfloat16 [24576, 3072], P('ctx', 'head')
- value_grads: bfloat16 [24576, 3072], P('ctx', 'head')
Inputs may be any that keep to these rules, and one draw needn't show every extreme that they name: `pattern`: row t lists distinct tiles whose frame tile (tile // 4) differs from that of t by at most one; t itself is always listed; -1 marks an empty slot and empty slots come last; three or more tiles are listed in every row.
All inputs are finite; a program needn't handle non-finite values.
Results may differ from a plain program's by a relative error of at most 0.035.
Values may be sent and summed in bfloat16 or wider, within the bound.
No kernel may reach another device: no remote copies, remote signals or barrier semaphores. Data moves between devices by JAX's collectives and lax.ppermute only.
A program may use at most 256 MiB of HBM per device.

v0:
```python
import functools
import math

import jax
import jax.numpy as jnp
from jax import lax
from jax.experimental import pallas as pl
from jax.experimental.pallas import tpu as pltpu
from jax.sharding import PartitionSpec as P

HD = 128
TILE = 384
SPT = 4
KSLOT = 8
SCALE = 1.0 / math.sqrt(HD)
NT = (((1,), (1,)), ((), ()))
TN = (((0,), (0,)), ((), ()))


def with_halo(block, axis, dim):
    count = lax.axis_size(axis)
    forward = [(i, i + 1) for i in range(count - 1)]
    backward = [(target, source) for source, target in forward]
    low = lax.ppermute(block, axis, forward)
    high = lax.ppermute(block, axis, backward)
    return jnp.concatenate([low, block, high], axis=dim)


def from_behind(block, axis, distance):
    devices = range(lax.axis_size(axis))
    route = [(i - distance, i) for i in devices if i - distance in devices]
    return lax.ppermute(block, axis, route)


def attention_kernel(
    slots_ref, counts_ref, q_ref, do_ref, k_ref, v_ref,
    o_ref, dq_ref, dk_ref, dv_ref, s_scr,
):
    a = pl.program_id(1)

    @pl.when(a == 0)
    def _():
        dk_ref[...] = jnp.zeros_like(dk_ref)
        dv_ref[...] = jnp.zeros_like(dv_ref)

    q = q_ref[...]
    do = do_ref[...]
    count = counts_ref[a]

    def rows(s):
        start = pl.multiple_of(slots_ref[a * KSLOT + s] * TILE, TILE)
        return pl.ds(start, TILE)

    def score_pass(s, row_max):
        scores = lax.dot_general(
            q, k_ref[rows(s), :], NT, preferred_element_type=jnp.float32
        ) * SCALE
        s_scr[s] = scores
        return jnp.maximum(row_max, jnp.max(scores, axis=1, keepdims=True))

    row_max = lax.fori_loop(
        0, count, score_pass, jnp.full((TILE, 1), -jnp.inf, jnp.float32)
    )

    def exp_pass(s, row_total):
        e = jnp.exp(s_scr[s] - row_max)
        s_scr[s] = e
        return row_total + jnp.sum(e, axis=1, keepdims=True)

    row_total = lax.fori_loop(0, count, exp_pass, jnp.zeros((TILE, 1), jnp.float32))
    inv_total = 1.0 / row_total

    def value_pass(s, acc):
        w = (s_scr[s] * inv_total).astype(jnp.bfloat16)
        return acc + jnp.dot(w, v_ref[rows(s), :], preferred_element_type=jnp.float32)

    out = lax.fori_loop(0, count, value_pass, jnp.zeros((TILE, HD), jnp.float32))
    out = out.astype(jnp.bfloat16)
    o_ref[...] = out
    delta = jnp.sum(do.astype(jnp.float32) * out.astype(jnp.float32), axis=1, keepdims=True)

    def grad_pass(s, dq_acc):
        r = rows(s)
        w = s_scr[s] * inv_total
        g = lax.dot_general(do, v_ref[r, :], NT, preferred_element_type=jnp.float32)
        ds = (w * (g - delta)).astype(jnp.bfloat16)
        dk_ref[r, :] += lax.dot_general(ds, q, TN, preferred_element_type=jnp.float32)
        dv_ref[r, :] += lax.dot_general(
            w.astype(jnp.bfloat16), do, TN, preferred_element_type=jnp.float32
        )
        return dq_acc + jnp.dot(ds, k_ref[r, :], preferred_element_type=jnp.float32)

    dq = lax.fori_loop(0, count, grad_pass, jnp.zeros((TILE, HD), jnp.float32))
    dq_ref[...] = (dq * SCALE).astype(jnp.bfloat16)


def attention(slots, counts, queries, grads, keys, values):
    row_count, col_count = queries.shape
    heads = col_count // HD
    tiles = row_count // TILE
    ext_rows = keys.shape[0]
    tile_spec = pl.BlockSpec((TILE, HD), lambda h, a, sl, ct: (a, h))
    ext_spec = pl.BlockSpec((ext_rows, HD), lambda h, a, sl, ct: (0, h))
    return pl.pallas_call(
        attention_kernel,
        grid_spec=pltpu.PrefetchScalarGridSpec(
            num_scalar_prefetch=2,
            grid=(heads, tiles),
            in_specs=[tile_spec, tile_spec, ext_spec, ext_spec],
            out_specs=[tile_spec, tile_spec, ext_spec, ext_spec],
            scratch_shapes=[pltpu.VMEM((KSLOT, TILE, TILE), jnp.float32)],
        ),
        out_shape=[
            jax.ShapeDtypeStruct((row_count, col_count), jnp.bfloat16),
            jax.ShapeDtypeStruct((row_count, col_count), jnp.bfloat16),
            jax.ShapeDtypeStruct((ext_rows, col_count), jnp.float32),
            jax.ShapeDtypeStruct((ext_rows, col_count), jnp.float32),
        ],
        compiler_params=pltpu.CompilerParams(
            dimension_semantics=("arbitrary", "arbitrary"),
            vmem_limit_bytes=48 * 1024 * 1024,
        ),
    )(slots, counts, queries, grads, keys, values)


def shards(queries, key_states, value_states, out_grads, pattern):
    row_count, col_count = queries.shape
    own_tiles = row_count // TILE
    first_tile = lax.axis_index("ctx") * own_tiles
    base_tile = first_tile - SPT
    grads_heads = lax.all_to_all(out_grads, "head", split_axis=1, concat_axis=0, tiled=True)
    rims = with_halo(jnp.stack((key_states, value_states)), "ctx", 1)
    listed = lax.dynamic_slice_in_dim(pattern, first_tile, own_tiles, 0)
    allowed = listed >= 0
    slots = jnp.where(allowed, listed - base_tile, 0).reshape(-1).astype(jnp.int32)
    counts = jnp.sum(allowed.astype(jnp.int32), axis=1)
    out, dq, dk, dv = attention(slots, counts, queries, grads_heads, rims[0], rims[1])
    attended = lax.all_to_all(out, "head", split_axis=0, concat_axis=1, tiled=True)
    parts = jnp.stack((dk, dv))
    own_part = parts[:, row_count : 2 * row_count]
    lower_part = parts[:, :row_count].astype(jnp.bfloat16)
    upper_part = parts[:, 2 * row_count :].astype(jnp.bfloat16)
    from_above = from_behind(lower_part, "ctx", -1).astype(jnp.float32)
    from_below = from_behind(upper_part, "ctx", 1).astype(jnp.float32)
    total = own_part + from_above + from_below
    key_grads = (total[0] * SCALE).astype(jnp.bfloat16)
    value_grads = total[1].astype(jnp.bfloat16)
    return (attended, dq, key_grads, value_grads)


def solution(mesh):
    return jax.shard_map(
        shards,
        mesh=mesh,
        in_specs=(
            P("ctx", "head"),
            P("ctx", "head"),
            P("ctx", "head"),
            P(("ctx", "head"), None),
            P(),
        ),
        out_specs=(P(("ctx", "head"), None), P("ctx", "head"), P("ctx", "head"), P("ctx", "head")),
        check_vma=False,
    )
```

profile of v0, /device:TPU:33, one launch (start us, length us, event | category | flops | bytes accessed | tf_op | source)
XLA Modules:
  0.0 277.8 jit_solution(17775201492178944660)
XLA Ops:
  0.6 0.0 copy-start.3
  0.6 3.4 %pad_maximum_fusion.2 = bf16[2,1536,384]{2,1,0:T(8,128)(2,1)} fusion(bf16[1,1536,384]{2,1,0:T(8,128)(2,1)} %bitcast.29, bf16[1,1536,384]{2,1,0:T(8,128)(2,1)} %bitcast.31), kind=kLoop, calls=%fused_computation.13 | loop fusion | flops 1179648 | bytes 4718592 | tf_op jit(solution)/shard_map/stack | solution.py:132
  4.1 2.7 collective-permute-start.1
  6.8 3.0 %collective-permute-start = (bf16[2,1536,384]{2,1,0:T(8,128)(2,1)}, bf16[2,1536,384]{2,1,0:T(8,128)(2,1)}, u32[]{:S(2)}, u32[]{:S(2)}) collective-permute-start(bf16[2,1536,384]{2,1,0:T(8,128)(2,1)} %pad_maximum_fusion.2), channel_id=1, source_target_pairs={{0,8},{8,16},{16,24},{24,32},{32,40},{40,48},{48,56},{56,64},{64,7... | collective-permute-start | bytes 7077896 | tf_op jit(solution)/shard_map/ppermute | solution.py:24
  9.8 0.0 copy-done.3
  9.8 1.1 copy.15
  10.9 6.6 %all-to-all-start = ((bf16[192,8,384]{2,0,1:T(8,128)(2,1)}), bf16[192,8,384]{2,0,1:T(8,128)(2,1)S(1)}, u32[]{:S(2)}, u32[]{:S(2)}) async-start(bf16[192,8,384]{2,0,1:T(8,128)(2,1)} %bitcast.33), calls=%async_computation | async-start | bytes 2359296 | tf_op jit(solution)/shard_map/all_to_all | solution.py:131
  17.6 0.0 copy-done.4
  17.6 0.1 convert_reduce_fusion
  17.7 0.1 subtract_select_fusion
  17.7 0.1 copy.9
  17.8 0.1 reshape.21.slots_ref
  17.9 38.7 %collective-permute-done.1 = bf16[2,1536,384]{2,1,0:T(8,128)(2,1)} collective-permute-done((bf16[2,1536,384]{2,1,0:T(8,128)(2,1)}, bf16[2,1536,384]{2,1,0:T(8,128)(2,1)}, u32[]{:S(2)}, u32[]{:S(2)}) %collective-permute-start.1) | collective-permute-done | bytes 2359328 | tf_op jit(solution)/shard_map/ppermute | solution.py:25
  56.6 4.6 %collective-permute-done = bf16[2,1536,384]{2,1,0:T(8,128)(2,1)} collective-permute-done((bf16[2,1536,384]{2,1,0:T(8,128)(2,1)}, bf16[2,1536,384]{2,1,0:T(8,128)(2,1)}, u32[]{:S(2)}, u32[]{:S(2)}) %collective-permute-start) | collective-permute-done | bytes 2359328 | tf_op jit(solution)/shard_map/ppermute | solution.py:24
  61.2 0.0 copy-done.1
  61.2 0.0 copy-done.2
  61.2 3.6 %pad_maximum_fusion.1 = bf16[2,4608,384]{2,1,0:T(8,128)(2,1)S(1)} fusion(bf16[2,1536,384]{2,1,0:T(8,128)(2,1)} %collective-permute-done.1, bf16[1,1536,384]{2,1,0:T(8,128)(2,1)S(1)} %bitcast.30, bf16[1,1536,384]{2,1,0:T(8,128)(2,1)S(1)} %bitcast.32, bf16[2,1536,384]{2,1,0:T(8,128)(2,1)} %collective-permute-done), kind=kLoop, calls=%fused_computation.4 | loop fusion | flops 28311552 | bytes 14155776 | tf_op jit(solution)/shard_map/concatenate | solution.py:26
  64.8 0.0 copy-start
  64.8 3.5 %slice_bitcast_fusion = (bf16[4608,384]{1,0:T(8,128)(2,1)}, bf16[4608,384]{1,0:T(8,128)(2,1)}) fusion(bf16[2,4608,384]{2,1,0:T(8,128)(2,1)S(1)} %pad_maximum_fusion.1), kind=kLoop, calls=%fused_computation.8 | loop fusion | bytes 14155776 | tf_op jit(solution)/shard_map/squeeze | solution.py:137
  68.3 8.4 %all-to-all-done = bf16[192,8,384]{2,0,1:T(8,128)(2,1)S(1)} async-done(((bf16[192,8,384]{2,0,1:T(8,128)(2,1)}), bf16[192,8,384]{2,0,1:T(8,128)(2,1)S(1)}, u32[]{:S(2)}, u32[]{:S(2)}) %all-to-all-start) | async-done | bytes 1179680 | tf_op jit(solution)/shard_map/all_to_all | solution.py:131
  76.7 87.0 %shard_map.84 = (bf16[1536,384]{1,0:T(8,128)(2,1)S(1)}, bf16[1536,384]{1,0:T(8,128)(2,1)}, f32[4608,384]{1,0:T(8,128)}, f32[4608,384]{1,0:T(8,128)}) custom-call(s32[32]{0:T(128)S(1)} %reshape.21.slots_ref, s32[4]{0:T(128)S(1)} %get-tuple-element.12.counts_ref, bf16[1536,384]{1,0:T(8,128)(2,1)S(1)} %copy-done, bf16[1536,384]{1,0:T(8,128)(2,1)S(1)} %bitcast.23, ...), custom_call_target="tpu_custom_call" | custom-call | tf_op jit(solution)/shard_map/pallas_call | solution.py:104
  163.7 8.8 %fusion = bf16[2,4608,384]{2,1,0:T(8,128)(2,1)} fusion(f32[1,4608,384]{2,1,0:T(8,128)} %bitcast.27, f32[1,4608,384]{2,1,0:T(8,128)} %bitcast.25), kind=kLoop, calls=%fused_computation.3 | loop fusion | flops 3538944 | bytes 21233664 | tf_op jit(solution)/shard_map/convert.2
  172.5 2.8 %fusion.7 = (bf16[2,1536,384]{2,1,0:T(8,128)(2,1)S(1)}, bf16[2,1536,384]{2,1,0:T(8,128)(2,1)S(1)}) fusion(bf16[2,4608,384]{2,1,0:T(8,128)(2,1)} %fusion), kind=kLoop, calls=%fused_computation.20 | loop fusion | bytes 9437184 | tf_op jit(solution)/shard_map/slice | solution.py:141
  175.4 30.1 %collective-permute-start.2 = (bf16[2,1536,384]{2,1,0:T(8,128)(2,1)S(1)}, bf16[2,1536,384]{2,1,0:T(8,128)(2,1)S(1)}, u32[]{:S(2)}, u32[]{:S(2)}) collective-permute-start(bf16[2,1536,384]{2,1,0:T(8,128)(2,1)S(1)} %get-tuple-element.14), channel_id=1, source_target_pairs={{8,0},{16,8},{24,16},{32,24},{40,32},{48,40},{56,48},{64,56},{72,6... | collective-permute-start | bytes 7077896 | tf_op jit(solution)/shard_map/ppermute | solution.py:32
  205.4 1.9 collective-permute-start.3
  207.4 63.6 %all_to_all.38 = bf16[8,192,384]{2,1,0:T(8,128)(2,1)S(1)} all-to-all(bf16[8,192,384]{2,1,0:T(8,128)(2,1)S(1)} %bitcast.24), channel_id=1, replica_groups=mesh['ctx'=16,'head'=8] {'head'}, dimensions={0} | all-to-all | bytes 2359296 | tf_op jit(solution)/shard_map/all_to_all | solution.py:138
  271.0 1.2 copy.13
  272.2 0.0 collective-permute-done.2
  272.2 0.0 collective-permute-done.3
  272.2 3.2 %fusion.3 = f32[2,1536,384]{2,1,0:T(8,128)S(1)} fusion(f32[1,4608,384]{2,1,0:T(8,128)} %bitcast.26, f32[1,4608,384]{2,1,0:T(8,128)} %bitcast.28, bf16[2,1536,384]{2,1,0:T(8,128)(2,1)S(1)} %collective-permute-done.3, bf16[2,1536,384]{2,1,0:T(8,128)(2,1)S(1)} %collective-permute-done.2), kind=kLoop, calls=%fused_computation.7 | loop fusion | flops 5898240 | bytes 23592960 | tf_op jit(solution)/shard_map/add | solution.py:145
  275.4 1.1 fusion.6
  276.6 1.3 fusion.5
  (4 shorter events, 0.0 us)
Async XLA Ops:
  0.6 9.2 %copy-start.3 = (bf16[192,3072]{1,0:T(8,128)(2,1)S(1)}, bf16[192,3072]{1,0:T(8,128)(2,1)}, u32[]{:S(2)}) copy-start(bf16[192,3072]{1,0:T(8,128)(2,1)} %param.8) | copy-start | bytes 3538948
  4.0 13.5 %copy-start.4 = (s32[64,8]{0,1:T(8,128)S(1)}, s32[64,8]{0,1:T(8,128)}, u32[]{:S(2)}) copy-start(s32[64,8]{0,1:T(8,128)} %param.9) | copy-start | bytes 6148
  4.0 57.1 %copy-start.1 = (bf16[1536,384]{1,0:T(8,128)(2,1)S(1)}, bf16[1536,384]{1,0:T(8,128)(2,1)}, u32[]{:S(2)}) copy-start(bf16[1536,384]{1,0:T(8,128)(2,1)} %param.7) | copy-start | bytes 3538948
  4.1 57.1 %copy-start.2 = (bf16[1536,384]{1,0:T(8,128)(2,1)S(1)}, bf16[1536,384]{1,0:T(8,128)(2,1)}, u32[]{:S(2)}) copy-start(bf16[1536,384]{1,0:T(8,128)(2,1)} %param.6) | copy-start | bytes 3538948
  4.1 52.5 %collective-permute-start.1 = (bf16[2,1536,384]{2,1,0:T(8,128)(2,1)}, bf16[2,1536,384]{2,1,0:T(8,128)(2,1)}, u32[]{:S(2)}, u32[]{:S(2)}) collective-permute-start(bf16[2,1536,384]{2,1,0:T(8,128)(2,1)} %pad_maximum_fusion.2), channel_id=1, source_target_pairs={{8,0},{16,8},{24,16},{32,24},{40,32},{48,40},{56,48},{64,56},{72,6... | collective-permute-start | bytes 7077896 | tf_op jit(solution)/shard_map/ppermute | solution.py:25
  6.8 54.4 %collective-permute-start = (bf16[2,1536,384]{2,1,0:T(8,128)(2,1)}, bf16[2,1536,384]{2,1,0:T(8,128)(2,1)}, u32[]{:S(2)}, u32[]{:S(2)}) collective-permute-start(bf16[2,1536,384]{2,1,0:T(8,128)(2,1)} %pad_maximum_fusion.2), channel_id=1, source_target_pairs={{0,8},{8,16},{16,24},{24,32},{32,40},{40,48},{48,56},{56,64},{64,7... | collective-permute-start | bytes 7077896 | tf_op jit(solution)/shard_map/ppermute | solution.py:24
  10.9 65.7 %all-to-all-start = ((bf16[192,8,384]{2,0,1:T(8,128)(2,1)}), bf16[192,8,384]{2,0,1:T(8,128)(2,1)S(1)}, u32[]{:S(2)}, u32[]{:S(2)}) async-start(bf16[192,8,384]{2,0,1:T(8,128)(2,1)} %bitcast.33), calls=%async_computation | async-start | bytes 2359296 | tf_op jit(solution)/shard_map/all_to_all | solution.py:131
  64.8 11.9 %copy-start = (bf16[1536,384]{1,0:T(8,128)(2,1)S(1)}, bf16[1536,384]{1,0:T(8,128)(2,1)}, u32[]{:S(2)}) copy-start(bf16[1536,384]{1,0:T(8,128)(2,1)} %q_ref.1) | copy-start | bytes 3538948
  175.4 96.8 %collective-permute-start.2 = (bf16[2,1536,384]{2,1,0:T(8,128)(2,1)S(1)}, bf16[2,1536,384]{2,1,0:T(8,128)(2,1)S(1)}, u32[]{:S(2)}, u32[]{:S(2)}) collective-permute-start(bf16[2,1536,384]{2,1,0:T(8,128)(2,1)S(1)} %get-tuple-element.14), channel_id=1, source_target_pairs={{8,0},{16,8},{24,16},{32,24},{40,32},{48,40},{56,48},{64,56},{72,6... | collective-permute-start | bytes 7077896 | tf_op jit(solution)/shard_map/ppermute | solution.py:32
  205.4 66.8 %collective-permute-start.3 = (bf16[2,1536,384]{2,1,0:T(8,128)(2,1)S(1)}, bf16[2,1536,384]{2,1,0:T(8,128)(2,1)S(1)}, u32[]{:S(2)}, u32[]{:S(2)}) collective-permute-start(bf16[2,1536,384]{2,1,0:T(8,128)(2,1)S(1)} %get-tuple-element.15), channel_id=1, source_target_pairs={{0,8},{8,16},{16,24},{24,32},{32,40},{40,48},{48,56},{56,64},{64,7... | collective-permute-start | bytes 7077896 | tf_op jit(solution)/shard_map/ppermute | solution.py:32
where the time goes:
time: 278 us
  Pallas kernels  87 us (31%)
  blocking collectives  63.6 us (23%)
  waiting for transfers between devices  51.6 us (19%)
  starting transfers between devices  44.3 us (16%)
  other arithmetic  20.5 us (7%)
  local copies, waits for them, and re-layouts  10.1 us (4%)
    pallas_call x1, Pallas kernels, attention(): pl.pallas_call(attention_kernel, grid_spec=pltpu.PrefetchScalarGridSpec(n...  87 us
    all_to_all x1, blocking collectives, shards(): lax.all_to_all(out, 'head', split_axis=0, concat_axis=1, tiled=True)  63.6 us
    ppermute x1, waiting for transfers between devices, with_halo(): high = lax.ppermute(block, axis, backward)  38.7 us
    ppermute x2, starting transfers between devices, from_behind(): return lax.ppermute(block, axis, route)  32 us
    another operation x1, other arithmetic  8.82 us
    all_to_all x1, waiting for transfers between devices, shards(): lax.all_to_all(out_grads, 'head', split_axis=1, concat_axis=0, tiled=True)  8.37 us
    all_to_all x1, starting transfers between devices, shards(): lax.all_to_all(out_grads, 'head', split_axis=1, concat_axis=0, tiled=True)  6.61 us
  transfers between devices with their start and end apart: 5, of which 3 were waited for; matrix products, arithmetic and copies ran while one was open for 4% of the time, Pallas kernels for 0%

commit v1 on v0

--- a/solution.py
+++ b/solution.py
@@ -36,7 +36,7 @@
     slots_ref, counts_ref, q_ref, do_ref, k_ref, v_ref,
     o_ref, dq_ref, dk_ref, dv_ref, s_scr,
 ):
-    a = pl.program_id(1)
+    a = pl.program_id(0)
 
     @pl.when(a == 0)
     def _():
@@ -94,30 +94,30 @@
     dq_ref[...] = (dq * SCALE).astype(jnp.bfloat16)
 
 
-def attention(slots, counts, queries, grads, keys, values):
-    row_count, col_count = queries.shape
-    heads = col_count // HD
+def attention(slots, counts, queries, grads, keys, values, head):
+    row_count = queries.shape[0]
     tiles = row_count // TILE
     ext_rows = keys.shape[0]
-    tile_spec = pl.BlockSpec((TILE, HD), lambda h, a, sl, ct: (a, h))
-    ext_spec = pl.BlockSpec((ext_rows, HD), lambda h, a, sl, ct: (0, h))
+    in_spec = pl.BlockSpec((TILE, HD), lambda a, sl, ct: (a, head))
+    tile_spec = pl.BlockSpec((TILE, HD), lambda a, sl, ct: (a, 0))
+    ext_spec = pl.BlockSpec((ext_rows, HD), lambda a, sl, ct: (0, 0))
     return pl.pallas_call(
         attention_kernel,
         grid_spec=pltpu.PrefetchScalarGridSpec(
             num_scalar_prefetch=2,
-            grid=(heads, tiles),
-            in_specs=[tile_spec, tile_spec, ext_spec, ext_spec],
+            grid=(tiles,),
+            in_specs=[in_spec, in_spec, ext_spec, ext_spec],
             out_specs=[tile_spec, tile_spec, ext_spec, ext_spec],
             scratch_shapes=[pltpu.VMEM((KSLOT, TILE, TILE), jnp.float32)],
         ),
         out_shape=[
-            jax.ShapeDtypeStruct((row_count, col_count), jnp.bfloat16),
-            jax.ShapeDtypeStruct((row_count, col_count), jnp.bfloat16),
-            jax.ShapeDtypeStruct((ext_rows, col_count), jnp.float32),
-            jax.ShapeDtypeStruct((ext_rows, col_count), jnp.float32),
+            jax.ShapeDtypeStruct((row_count, HD), jnp.bfloat16),
+            jax.ShapeDtypeStruct((row_count, HD), jnp.bfloat16),
+            jax.ShapeDtypeStruct((ext_rows, HD), jnp.float32),
+            jax.ShapeDtypeStruct((ext_rows, HD), jnp.float32),
         ],
         compiler_params=pltpu.CompilerParams(
-            dimension_semantics=("arbitrary", "arbitrary"),
+            dimension_semantics=("arbitrary",),
             vmem_limit_bytes=48 * 1024 * 1024,
         ),
     )(slots, counts, queries, grads, keys, values)
@@ -125,27 +125,41 @@
 
 def shards(queries, key_states, value_states, out_grads, pattern):
     row_count, col_count = queries.shape
+    heads = col_count // HD
     own_tiles = row_count // TILE
     first_tile = lax.axis_index("ctx") * own_tiles
     base_tile = first_tile - SPT
     grads_heads = lax.all_to_all(out_grads, "head", split_axis=1, concat_axis=0, tiled=True)
-    rims = with_halo(jnp.stack((key_states, value_states)), "ctx", 1)
     listed = lax.dynamic_slice_in_dim(pattern, first_tile, own_tiles, 0)
     allowed = listed >= 0
     slots = jnp.where(allowed, listed - base_tile, 0).reshape(-1).astype(jnp.int32)
     counts = jnp.sum(allowed.astype(jnp.int32), axis=1)
-    out, dq, dk, dv = attention(slots, counts, queries, grads_heads, rims[0], rims[1])
+    outs, dqs, dks, dvs = [], [], [], []
+    first = jnp.stack((key_states[:, :HD], value_states[:, :HD]))
+    rest = jnp.stack((key_states[:, HD:], value_states[:, HD:]))
+    halos = [with_halo(first, "ctx", 1), with_halo(rest, "ctx", 1)]
+    for h in range(heads):
+        cols = slice(h * HD, (h + 1) * HD)
+        rims = halos[0] if h == 0 else halos[1][:, :, (h - 1) * HD : h * HD]
+        with jax.named_scope(f"attention_head{h}"):
+            out, dq, dk, dv = attention(
+                slots, counts, queries, grads_heads, rims[0], rims[1], h
+            )
+        parts = jnp.stack((dk, dv))
+        own_part = parts[:, row_count : 2 * row_count]
+        lower_part = parts[:, :row_count].astype(jnp.bfloat16)
+        upper_part = parts[:, 2 * row_count :].astype(jnp.bfloat16)
+        from_above = from_behind(lower_part, "ctx", -1).astype(jnp.float32)
+        from_below = from_behind(upper_part, "ctx", 1).astype(jnp.float32)
+        total = own_part + from_above + from_below
+        outs.append(out)
+        dqs.append(dq)
+        dks.append((total[0] * SCALE).astype(jnp.bfloat16))
+        dvs.append(total[1].astype(jnp.bfloat16))
+    out = jnp.concatenate(outs, axis=1)
     attended = lax.all_to_all(out, "head", split_axis=0, concat_axis=1, tiled=True)
-    parts = jnp.stack((dk, dv))
-    own_part = parts[:, row_count : 2 * row_count]
-    lower_part = parts[:, :row_count].astype(jnp.bfloat16)
-    upper_part = parts[:, 2 * row_count :].astype(jnp.bfloat16)
-    from_above = from_behind(lower_part, "ctx", -1).astype(jnp.float32)
-    from_below = from_behind(upper_part, "ctx", 1).astype(jnp.float32)
-    total = own_part + from_above + from_below
-    key_grads = (total[0] * SCALE).astype(jnp.bfloat16)
-    value_grads = total[1].astype(jnp.bfloat16)
-    return (attended, dq, key_grads, value_grads)
+    cat = functools.partial(jnp.concatenate, axis=1)
+    return (attended, cat(dqs), cat(dks), cat(dvs))
 
 
 def solution(mesh):

time: 278 us -> 271 us (0.975)
  the two profiles are of different devices: /device:TPU:33 before, /device:TPU:32 now
where the time goes in v1:
time: 271 us; the launch traced here: 269 us
  Pallas kernels  94.3 us (35%)
  waiting for transfers between devices  70.3 us (26%)
  starting transfers between devices  68.2 us (25%)
  other arithmetic  23.4 us (9%)
  local copies, waits for them, and re-layouts  11.8 us (4%)
    pallas_call x3, Pallas kernels, attention(): pl.pallas_call(attention_kernel, grid_spec=pltpu.PrefetchScalarGridSpec(n...  94.3 us
    all_to_all x1, waiting for transfers between devices, shards(): lax.all_to_all(out_grads, 'head', split_axis=1, concat_axis=0, tiled=True)  46.9 us
    ppermute x6, starting transfers between devices, from_behind(): return lax.ppermute(block, axis, route)  44.8 us
    ppermute x6, waiting for transfers between devices, from_behind(): return lax.ppermute(block, axis, route)  21.6 us
    ppermute x2, starting transfers between devices, with_halo(): high = lax.ppermute(block, axis, backward)  9.08 us
    another operation x3, other arithmetic  8.48 us
    all_to_all x1, starting transfers between devices, shards(): lax.all_to_all(out_grads, 'head', split_axis=1, concat_axis=0, tiled=True)  6.93 us
  transfers between devices with their start and end apart: 12, of which 4 were waited for; matrix products, arithmetic and copies ran while one was open for 11% of the time, Pallas kernels for 35%

profile of v1, /device:TPU:32, one launch (start us, length us, event | category | flops | bytes accessed | tf_op | source)
XLA Modules:
  0.0 269.0 jit_solution(9172446161468961144)
XLA Ops:
  0.7 1.3 slice_bitcast_fusion.8
  2.9 1.9 collective-permute-start
  4.8 4.5 %collective-permute-start.1 = (bf16[2,1536,128]{2,1,0:T(8,128)(2,1)}, bf16[2,1536,128]{2,1,0:T(8,128)(2,1)S(1)}, u32[]{:S(2)}, u32[]{:S(2)}) collective-permute-start(bf16[2,1536,128]{2,1,0:T(8,128)(2,1)} %pad_maximum_fusion.10), channel_id=1, source_target_pairs={{8,0},{16,8},{24,16},{32,24},{40,32},{48,40},{56,48},{64,56},{72,6... | collective-permute-start | bytes 2359304 | tf_op jit(solution)/shard_map/ppermute | solution.py:25
  9.6 1.4 pad_maximum_fusion.5
  10.9 1.9 collective-permute-start.2
  12.8 4.5 %collective-permute-start.3 = (bf16[2,1536,256]{2,1,0:T(8,128)(2,1)}, bf16[2,1536,256]{2,1,0:T(8,128)(2,1)}, u32[]{:S(2)}, u32[]{:S(2)}) collective-permute-start(bf16[2,1536,256]{2,1,0:T(8,128)(2,1)} %pad_maximum_fusion.5), channel_id=1, source_target_pairs={{8,0},{16,8},{24,16},{32,24},{40,32},{48,40},{56,48},{64,56},{72,6... | collective-permute-start | bytes 4718600 | tf_op jit(solution)/shard_map/ppermute | solution.py:25
  18.5 6.9 %all-to-all-start = ((bf16[192,8,384]{2,0,1:T(8,128)(2,1)}), bf16[192,8,384]{2,0,1:T(8,128)(2,1)S(1)}, u32[]{:S(2)}, u32[]{:S(2)}) async-start(bf16[192,8,384]{2,0,1:T(8,128)(2,1)} %bitcast.48), calls=%async_computation | async-start | bytes 2359296 | tf_op jit(solution)/shard_map/all_to_all | solution.py:132
  25.8 1.8 collective-permute-done.1
  28.9 46.9 %all-to-all-done = bf16[192,8,384]{2,0,1:T(8,128)(2,1)S(1)} async-done(((bf16[192,8,384]{2,0,1:T(8,128)(2,1)}), bf16[192,8,384]{2,0,1:T(8,128)(2,1)S(1)}, u32[]{:S(2)}, u32[]{:S(2)}) %all-to-all-start) | async-done | bytes 1179680 | tf_op jit(solution)/shard_map/all_to_all | solution.py:132
  75.9 1.3 copy-done.1
  77.1 31.4 %attention_head0.1 = (bf16[1536,128]{1,0:T(8,128)(2,1)S(1)}, bf16[1536,128]{1,0:T(8,128)(2,1)S(1)}, f32[4608,128]{1,0:T(8,128)}, f32[4608,128]{1,0:T(8,128)}) custom-call(s32[32]{0:T(128)S(1)} %reshape.29.slots_ref, s32[4]{0:T(128)S(1)} %get-tuple-element.28.counts_ref, bf16[1536,384]{1,0:T(8,128)(2,1)S(1)} %copy-done, bf16[1536,384]{1,0:T(8,128)(2,1)S(1)} %bitcast.49, ...), custom_call_target="tpu_custom_call" | custom-call | tf_op jit(solution)/shard_map/attention_head0/pallas_call | solution.py:104
  108.5 2.9 %fusion.2 = bf16[2,4608,128]{2,1,0:T(8,128)(2,1)S(1)} fusion(f32[1,4608,128]{2,1,0:T(8,128)} %bitcast.54, f32[1,4608,128]{2,1,0:T(8,128)} %bitcast.52), kind=kLoop, calls=%fused_computation.11 | loop fusion | flops 1179648 | bytes 7077888 | tf_op jit(solution)/shard_map/convert.8
  111.5 1.2 fusion.21
  112.7 9.0 %collective-permute-start.4 = (bf16[2,1536,128]{2,1,0:T(8,128)(2,1)}, bf16[2,1536,128]{2,1,0:T(8,128)(2,1)}, u32[]{:S(2)}, u32[]{:S(2)}) collective-permute-start(bf16[2,1536,128]{2,1,0:T(8,128)(2,1)} %get-tuple-element.34), channel_id=1, source_target_pairs={{8,0},{16,8},{24,16},{32,24},{40,32},{48,40},{56,48},{64,56},{72,6... | collective-permute-start | bytes 2359304 | tf_op jit(solution)/shard_map/ppermute | solution.py:32
  121.7 1.9 collective-permute-start.5
  123.7 2.3 pad_maximum_fusion.3
  126.8 31.4 %attention_head1.1 = (bf16[1536,128]{1,0:T(8,128)(2,1)S(1)}, bf16[1536,128]{1,0:T(8,128)(2,1)S(1)}, f32[4608,128]{1,0:T(8,128)}, f32[4608,128]{1,0:T(8,128)}) custom-call(s32[32]{0:T(128)S(1)} %reshape.29.slots_ref, s32[4]{0:T(128)S(1)} %get-tuple-element.28.counts_ref, bf16[1536,384]{1,0:T(8,128)(2,1)S(1)} %copy-done, bf16[1536,384]{1,0:T(8,128)(2,1)S(1)} %bitcast.50, ...), custom_call_target="tpu_custom_call" | custom-call | tf_op jit(solution)/shard_map/attention_head1/pallas_call | solution.py:104
  158.2 2.8 %fusion.1 = bf16[2,4608,128]{2,1,0:T(8,128)(2,1)S(1)} fusion(f32[1,4608,128]{2,1,0:T(8,128)} %bitcast.58, f32[1,4608,128]{2,1,0:T(8,128)} %bitcast.56), kind=kLoop, calls=%fused_computation.10 | loop fusion | flops 1179648 | bytes 7077888 | tf_op jit(solution)/shard_map/convert.6
  161.0 1.3 fusion.22
  162.3 16.1 %collective-permute-start.6 = (bf16[2,1536,128]{2,1,0:T(8,128)(2,1)}, bf16[2,1536,128]{2,1,0:T(8,128)(2,1)}, u32[]{:S(2)}, u32[]{:S(2)}) collective-permute-start(bf16[2,1536,128]{2,1,0:T(8,128)(2,1)} %get-tuple-element.36), channel_id=1, source_target_pairs={{8,0},{16,8},{24,16},{32,24},{40,32},{48,40},{56,48},{64,56},{72,6... | collective-permute-start | bytes 2359304 | tf_op jit(solution)/shard_map/ppermute | solution.py:32
  178.4 1.9 collective-permute-start.7
  180.3 31.5 %attention_head2.1 = (bf16[1536,128]{1,0:T(8,128)(2,1)S(1)}, bf16[1536,128]{1,0:T(8,128)(2,1)S(1)}, f32[4608,128]{1,0:T(8,128)}, f32[4608,128]{1,0:T(8,128)}) custom-call(s32[32]{0:T(128)S(1)} %reshape.29.slots_ref, s32[4]{0:T(128)S(1)} %get-tuple-element.28.counts_ref, bf16[1536,384]{1,0:T(8,128)(2,1)S(1)} %copy-done, bf16[1536,384]{1,0:T(8,128)(2,1)S(1)} %bitcast.51, ...), custom_call_target="tpu_custom_call" | custom-call | tf_op jit(solution)/shard_map/attention_head2/pallas_call | solution.py:104
  211.8 2.8 %fusion = bf16[2,4608,128]{2,1,0:T(8,128)(2,1)S(1)} fusion(f32[1,4608,128]{2,1,0:T(8,128)} %bitcast.62, f32[1,4608,128]{2,1,0:T(8,128)} %bitcast.60), kind=kLoop, calls=%fused_computation.9 | loop fusion | flops 1179648 | bytes 7077888 | tf_op jit(solution)/shard_map/convert.4
  215.6 13.9 %collective-permute-start.8 = (bf16[2,1536,128]{2,1,0:T(8,128)(2,1)}, bf16[2,1536,128]{2,1,0:T(8,128)(2,1)}, u32[]{:S(2)}, u32[]{:S(2)}) collective-permute-start(bf16[2,1536,128]{2,1,0:T(8,128)(2,1)} %get-tuple-element.38), channel_id=1, source_target_pairs={{8,0},{16,8},{24,16},{32,24},{40,32},{48,40},{56,48},{64,56},{72,6... | collective-permute-start | bytes 2359304 | tf_op jit(solution)/shard_map/ppermute | solution.py:32
  230.7 3.6 %all-to-all-start.1 = ((bf16[8,192,384]{2,1,0:T(8,128)(2,1)}), bf16[8,192,384]{2,1,0:T(8,128)(2,1)S(1)}, u32[]{:S(2)}, u32[]{:S(2)}) async-start(bf16[8,192,384]{2,1,0:T(8,128)(2,1)} %bitcast.65), calls=%async_computation.1 | async-start | bytes 2359296 | tf_op jit(solution)/shard_map/all_to_all | solution.py:160
  235.4 1.9 collective-permute-start.9
  237.4 2.0 fusion.11
  240.4 1.8 fusion.8
  242.3 4.2 %collective-permute-done.8 = bf16[2,1536,128]{2,1,0:T(8,128)(2,1)} collective-permute-done((bf16[2,1536,128]{2,1,0:T(8,128)(2,1)}, bf16[2,1536,128]{2,1,0:T(8,128)(2,1)}, u32[]{:S(2)}, u32[]{:S(2)}) %collective-permute-start.8) | collective-permute-done | bytes 786464 | tf_op jit(solution)/shard_map/ppermute | solution.py:32
  246.6 17.4 %collective-permute-done.9 = bf16[2,1536,128]{2,1,0:T(8,128)(2,1)S(1)} collective-permute-done((bf16[2,1536,128]{2,1,0:T(8,128)(2,1)S(1)}, bf16[2,1536,128]{2,1,0:T(8,128)(2,1)S(1)}, u32[]{:S(2)}, u32[]{:S(2)}) %collective-permute-start.9) | collective-permute-done | bytes 786464 | tf_op jit(solution)/shard_map/ppermute | solution.py:32
  264.0 1.4 fusion.5
  267.8 1.2 copy.13
  (62 shorter events, 11.7 us)
Async XLA Ops:
  0.6 8.8 %copy-start.15 = (bf16[1536,384]{1,0:T(8,128)(2,1)S(1)}, bf16[1536,384]{1,0:T(8,128)(2,1)}, u32[]{:S(2)}) copy-start(bf16[1536,384]{1,0:T(8,128)(2,1)} %param.6) | copy-start | bytes 3538948
  0.6 8.8 %copy-start.14 = (bf16[1536,384]{1,0:T(8,128)(2,1)S(1)}, bf16[1536,384]{1,0:T(8,128)(2,1)}, u32[]{:S(2)}) copy-start(bf16[1536,384]{1,0:T(8,128)(2,1)} %param.7) | copy-start | bytes 3538948
  2.9 22.9 %collective-permute-start = (bf16[2,1536,128]{2,1,0:T(8,128)(2,1)}, bf16[2,1536,128]{2,1,0:T(8,128)(2,1)S(1)}, u32[]{:S(2)}, u32[]{:S(2)}) collective-permute-start(bf16[2,1536,128]{2,1,0:T(8,128)(2,1)} %pad_maximum_fusion.10), channel_id=1, source_target_pairs={{0,8},{8,16},{16,24},{24,32},{32,40},{40,48},{48,56},{56,64},{64,7... | collective-permute-start | bytes 2359304 | tf_op jit(solution)/shard_map/ppermute | solution.py:24
  4.8 22.8 %collective-permute-start.1 = (bf16[2,1536,128]{2,1,0:T(8,128)(2,1)}, bf16[2,1536,128]{2,1,0:T(8,128)(2,1)S(1)}, u32[]{:S(2)}, u32[]{:S(2)}) collective-permute-start(bf16[2,1536,128]{2,1,0:T(8,128)(2,1)} %pad_maximum_fusion.10), channel_id=1, source_target_pairs={{8,0},{16,8},{24,16},{32,24},{40,32},{48,40},{56,48},{64,56},{72,6... | collective-permute-start | bytes 2359304 | tf_op jit(solution)/shard_map/ppermute | solution.py:25
  9.5 9.0 %copy-start.9 = (bf16[1,1536,256]{2,1,0:T(8,128)(2,1)}, bf16[1,1536,256]{2,1,0:T(8,128)(2,1)S(1)}, u32[]{:S(2)}) copy-start(bf16[1,1536,256]{2,1,0:T(8,128)(2,1)S(1)} %get-tuple-element.42) | copy-start | bytes 2359300
  9.5 9.0 %copy-start.11 = (bf16[1,1536,256]{2,1,0:T(8,128)(2,1)}, bf16[1,1536,256]{2,1,0:T(8,128)(2,1)S(1)}, u32[]{:S(2)}) copy-start(bf16[1,1536,256]{2,1,0:T(8,128)(2,1)S(1)} %get-tuple-element.43) | copy-start | bytes 2359300
  9.5 7.8 %copy-start.13 = (bf16[192,3072]{1,0:T(8,128)(2,1)S(1)}, bf16[192,3072]{1,0:T(8,128)(2,1)}, u32[]{:S(2)}) copy-start(bf16[192,3072]{1,0:T(8,128)(2,1)} %param.8) | copy-start | bytes 3538948
  10.9 112.7 %collective-permute-start.2 = (bf16[2,1536,256]{2,1,0:T(8,128)(2,1)}, bf16[2,1536,256]{2,1,0:T(8,128)(2,1)}, u32[]{:S(2)}, u32[]{:S(2)}) collective-permute-start(bf16[2,1536,256]{2,1,0:T(8,128)(2,1)} %pad_maximum_fusion.5), channel_id=1, source_target_pairs={{0,8},{8,16},{16,24},{24,32},{32,40},{40,48},{48,56},{56,64},{64,7... | collective-permute-start | bytes 4718600 | tf_op jit(solution)/shard_map/ppermute | solution.py:24
  12.8 110.8 %collective-permute-start.3 = (bf16[2,1536,256]{2,1,0:T(8,128)(2,1)}, bf16[2,1536,256]{2,1,0:T(8,128)(2,1)}, u32[]{:S(2)}, u32[]{:S(2)}) collective-permute-start(bf16[2,1536,256]{2,1,0:T(8,128)(2,1)} %pad_maximum_fusion.5), channel_id=1, source_target_pairs={{8,0},{16,8},{24,16},{32,24},{40,32},{48,40},{56,48},{64,56},{72,6... | collective-permute-start | bytes 4718600 | tf_op jit(solution)/shard_map/ppermute | solution.py:25
  17.4 8.1 %copy-start.16 = (s32[64,8]{0,1:T(8,128)S(1)}, s32[64,8]{0,1:T(8,128)}, u32[]{:S(2)}) copy-start(s32[64,8]{0,1:T(8,128)} %param.9) | copy-start | bytes 6148
  18.5 57.3 %all-to-all-start = ((bf16[192,8,384]{2,0,1:T(8,128)(2,1)}), bf16[192,8,384]{2,0,1:T(8,128)(2,1)S(1)}, u32[]{:S(2)}, u32[]{:S(2)}) async-start(bf16[192,8,384]{2,0,1:T(8,128)(2,1)} %bitcast.48), calls=%async_computation | async-start | bytes 2359296 | tf_op jit(solution)/shard_map/all_to_all | solution.py:132
  27.8 48.1 %copy-start = (bf16[1536,384]{1,0:T(8,128)(2,1)S(1)}, bf16[1536,384]{1,0:T(8,128)(2,1)}, u32[]{:S(2)}) copy-start(bf16[1536,384]{1,0:T(8,128)(2,1)} %q_ref.5) | copy-start | bytes 3538948
  75.8 1.3 copy-start.1
  108.5 2.9 %copy-start.2 = (bf16[1536,128]{1,0:T(8,128)(2,1)}, bf16[1536,128]{1,0:T(8,128)(2,1)S(1)}, u32[]{:S(2)}) copy-start(bf16[1536,128]{1,0:T(8,128)(2,1)S(1)} %get-tuple-element.19) | copy-start | bytes 1179652
  111.5 12.2 %copy-start.10 = (bf16[1,1536,256]{2,1,0:T(8,128)(2,1)S(1)}, bf16[1,1536,256]{2,1,0:T(8,128)(2,1)}, u32[]{:S(2)}) copy-start(bf16[1,1536,256]{2,1,0:T(8,128)(2,1)} %copy-done.9) | copy-start | bytes 2359300
  111.5 12.2 %copy-start.12 = (bf16[1,1536,256]{2,1,0:T(8,128)(2,1)S(1)}, bf16[1,1536,256]{2,1,0:T(8,128)(2,1)}, u32[]{:S(2)}) copy-start(bf16[1,1536,256]{2,1,0:T(8,128)(2,1)} %copy-done.11) | copy-start | bytes 2359300
  112.7 122.7 %collective-permute-start.4 = (bf16[2,1536,128]{2,1,0:T(8,128)(2,1)}, bf16[2,1536,128]{2,1,0:T(8,128)(2,1)}, u32[]{:S(2)}, u32[]{:S(2)}) collective-permute-start(bf16[2,1536,128]{2,1,0:T(8,128)(2,1)} %get-tuple-element.34), channel_id=1, source_target_pairs={{8,0},{16,8},{24,16},{32,24},{40,32},{48,40},{56,48},{64,56},{72,6... | collective-permute-start | bytes 2359304 | tf_op jit(solution)/shard_map/ppermute | solution.py:32
  121.7 115.6 %collective-permute-start.5 = (bf16[2,1536,128]{2,1,0:T(8,128)(2,1)}, bf16[2,1536,128]{2,1,0:T(8,128)(2,1)}, u32[]{:S(2)}, u32[]{:S(2)}) collective-permute-start(bf16[2,1536,128]{2,1,0:T(8,128)(2,1)} %get-tuple-element.35), channel_id=1, source_target_pairs={{0,8},{8,16},{16,24},{24,32},{32,40},{40,48},{48,56},{56,64},{64,7... | collective-permute-start | bytes 2359304 | tf_op jit(solution)/shard_map/ppermute | solution.py:32
  162.3 77.2 %collective-permute-start.6 = (bf16[2,1536,128]{2,1,0:T(8,128)(2,1)}, bf16[2,1536,128]{2,1,0:T(8,128)(2,1)}, u32[]{:S(2)}, u32[]{:S(2)}) collective-permute-start(bf16[2,1536,128]{2,1,0:T(8,128)(2,1)} %get-tuple-element.36), channel_id=1, source_target_pairs={{8,0},{16,8},{24,16},{32,24},{40,32},{48,40},{56,48},{64,56},{72,6... | collective-permute-start | bytes 2359304 | tf_op jit(solution)/shard_map/ppermute | solution.py:32
  178.4 61.1 %collective-permute-start.7 = (bf16[2,1536,128]{2,1,0:T(8,128)(2,1)}, bf16[2,1536,128]{2,1,0:T(8,128)(2,1)}, u32[]{:S(2)}, u32[]{:S(2)}) collective-permute-start(bf16[2,1536,128]{2,1,0:T(8,128)(2,1)} %get-tuple-element.37), channel_id=1, source_target_pairs={{0,8},{8,16},{16,24},{24,32},{32,40},{40,48},{48,56},{56,64},{64,7... | collective-permute-start | bytes 2359304 | tf_op jit(solution)/shard_map/ppermute | solution.py:32
  215.6 31.0 %collective-permute-start.8 = (bf16[2,1536,128]{2,1,0:T(8,128)(2,1)}, bf16[2,1536,128]{2,1,0:T(8,128)(2,1)}, u32[]{:S(2)}, u32[]{:S(2)}) collective-permute-start(bf16[2,1536,128]{2,1,0:T(8,128)(2,1)} %get-tuple-element.38), channel_id=1, source_target_pairs={{8,0},{16,8},{24,16},{32,24},{40,32},{48,40},{56,48},{64,56},{72,6... | collective-permute-start | bytes 2359304 | tf_op jit(solution)/shard_map/ppermute | solution.py:32
  229.5 4.8 %copy-start.3 = (bf16[1536,128]{1,0:T(8,128)(2,1)S(1)}, bf16[1536,128]{1,0:T(8,128)(2,1)}, u32[]{:S(2)}) copy-start(bf16[1536,128]{1,0:T(8,128)(2,1)} %copy-done.2) | copy-start | bytes 1179652
  230.7 37.2 %all-to-all-start.1 = ((bf16[8,192,384]{2,1,0:T(8,128)(2,1)}), bf16[8,192,384]{2,1,0:T(8,128)(2,1)S(1)}, u32[]{:S(2)}, u32[]{:S(2)}) async-start(bf16[8,192,384]{2,1,0:T(8,128)(2,1)} %bitcast.65), calls=%async_computation.1 | async-start | bytes 2359296 | tf_op jit(solution)/shard_map/all_to_all | solution.py:160
  234.2 3.1 %copy-start.4 = (f32[4608,128]{1,0:T(8,128)S(1)}, f32[4608,128]{1,0:T(8,128)}, u32[]{:S(2)}) copy-start(f32[4608,128]{1,0:T(8,128)} %get-tuple-element.22) | copy-start | bytes 7077892
  235.4 28.6 %collective-permute-start.9 = (bf16[2,1536,128]{2,1,0:T(8,128)(2,1)S(1)}, bf16[2,1536,128]{2,1,0:T(8,128)(2,1)S(1)}, u32[]{:S(2)}, u32[]{:S(2)}) collective-permute-start(bf16[2,1536,128]{2,1,0:T(8,128)(2,1)S(1)} %get-tuple-element.39), channel_id=1, source_target_pairs={{0,8},{8,16},{16,24},{24,32},{32,40},{40,48},{48,56},{56,64},{64,7... | collective-permute-start | bytes 2359304 | tf_op jit(solution)/shard_map/ppermute | solution.py:32
  237.4 2.4 copy-start.5
  237.4 3.1 %copy-start.6 = (f32[4608,128]{1,0:T(8,128)S(1)}, f32[4608,128]{1,0:T(8,128)}, u32[]{:S(2)}) copy-start(f32[4608,128]{1,0:T(8,128)} %get-tuple-element.25) | copy-start | bytes 7077892
  240.4 23.5 %copy-start.7 = (f32[4608,128]{1,0:T(8,128)S(1)}, f32[4608,128]{1,0:T(8,128)}, u32[]{:S(2)}) copy-start(f32[4608,128]{1,0:T(8,128)} %get-tuple-element.26) | copy-start | bytes 7077892
  240.4 23.5 %copy-start.8 = (f32[4608,128]{1,0:T(8,128)S(1)}, f32[4608,128]{1,0:T(8,128)}, u32[]{:S(2)}) copy-start(f32[4608,128]{1,0:T(8,128)} %get-tuple-element.27) | copy-start | bytes 7077892

commit v2 on v1

--- a/solution.py
+++ b/solution.py
@@ -99,6 +99,7 @@
     tiles = row_count // TILE
     ext_rows = keys.shape[0]
     in_spec = pl.BlockSpec((TILE, HD), lambda a, sl, ct: (a, head))
+    grad_spec = pl.BlockSpec((TILE, HD), lambda a, sl, ct: (a, 0))
     tile_spec = pl.BlockSpec((TILE, HD), lambda a, sl, ct: (a, 0))
     ext_spec = pl.BlockSpec((ext_rows, HD), lambda a, sl, ct: (0, 0))
     return pl.pallas_call(
@@ -106,7 +107,7 @@
         grid_spec=pltpu.PrefetchScalarGridSpec(
             num_scalar_prefetch=2,
             grid=(tiles,),
-            in_specs=[in_spec, in_spec, ext_spec, ext_spec],
+            in_specs=[in_spec, grad_spec, ext_spec, ext_spec],
             out_specs=[tile_spec, tile_spec, ext_spec, ext_spec],
             scratch_shapes=[pltpu.VMEM((KSLOT, TILE, TILE), jnp.float32)],
         ),
@@ -129,7 +130,16 @@
     own_tiles = row_count // TILE
     first_tile = lax.axis_index("ctx") * own_tiles
     base_tile = first_tile - SPT
-    grads_heads = lax.all_to_all(out_grads, "head", split_axis=1, concat_axis=0, tiled=True)
+    groups = lax.axis_size("head")
+    token_rows = out_grads.shape[0]
+    grads_split = out_grads.reshape(token_rows, groups, heads, HD)
+    grads_heads = [
+        lax.all_to_all(
+            grads_split[:, :, h].reshape(token_rows, groups * HD),
+            "head", split_axis=1, concat_axis=0, tiled=True,
+        )
+        for h in range(heads)
+    ]
     listed = lax.dynamic_slice_in_dim(pattern, first_tile, own_tiles, 0)
     allowed = listed >= 0
     slots = jnp.where(allowed, listed - base_tile, 0).reshape(-1).astype(jnp.int32)
@@ -143,7 +153,7 @@
         rims = halos[0] if h == 0 else halos[1][:, :, (h - 1) * HD : h * HD]
         with jax.named_scope(f"attention_head{h}"):
             out, dq, dk, dv = attention(
-                slots, counts, queries, grads_heads, rims[0], rims[1], h
+                slots, counts, queries, grads_heads[h], rims[0], rims[1], h
             )
         parts = jnp.stack((dk, dv))
         own_part = parts[:, row_count : 2 * row_count]
@@ -152,12 +162,13 @@
         from_above = from_behind(lower_part, "ctx", -1).astype(jnp.float32)
         from_below = from_behind(upper_part, "ctx", 1).astype(jnp.float32)
         total = own_part + from_above + from_below
-        outs.append(out)
+        outs.append(lax.all_to_all(out, "head", split_axis=0, concat_axis=1, tiled=True))
         dqs.append(dq)
         dks.append((total[0] * SCALE).astype(jnp.bfloat16))
         dvs.append(total[1].astype(jnp.bfloat16))
-    out = jnp.concatenate(outs, axis=1)
-    attended = lax.all_to_all(out, "head", split_axis=0, concat_axis=1, tiled=True)
+    attended = jnp.stack(
+        [o.reshape(token_rows, groups, HD) for o in outs], axis=2
+    ).reshape(token_rows, groups * heads * HD)
     cat = functools.partial(jnp.concatenate, axis=1)
     return (attended, cat(dqs), cat(dks), cat(dvs))
 

time: 271 us -> 295 us (1.089)
  the two profiles are of different devices: /device:TPU:32 before, /device:TPU:96 now
where the time goes in v2:
time: 295 us; the launch traced here: 292 us
  Pallas kernels  127 us (43%)
  starting transfers between devices  59 us (20%)
  waiting for transfers between devices  47.4 us (16%)
  local copies, waits for them, and re-layouts  32.9 us (11%)
  other arithmetic  24.2 us (8%)
    pallas_call x3, Pallas kernels, attention(): pl.pallas_call(attention_kernel, grid_spec=pltpu.PrefetchScalarGridSpec(n...  127 us
    all_to_all x3, waiting for transfers between devices, shards(): lax.all_to_all(grads_split[:, :, h].reshape(token_rows, groups * HD), 'he...  43.8 us
    all_to_all x3, starting transfers between devices, shards(): lax.all_to_all(out, 'head', split_axis=0, concat_axis=1, tiled=True)  17.9 us
    all_to_all x3, starting transfers between devices, shards(): lax.all_to_all(grads_split[:, :, h].reshape(token_rows, groups * HD), 'he...  17 us
    ppermute x6, starting transfers between devices, from_behind(): return lax.ppermute(block, axis, route)  13.1 us
    another operation x3, other arithmetic  8.81 us
    ppermute x2, starting transfers between devices, with_halo(): high = lax.ppermute(block, axis, backward)  7.2 us
    unnamed x50, local copies, waits for them, and re-layouts  6.29 us
  transfers between devices with their start and end apart: 16, of which 4 were waited for; matrix products, arithmetic and copies ran while one was open for 15% of the time, Pallas kernels for 44%

profile of v2, /device:TPU:96, one launch (start us, length us, event | category | flops | bytes accessed | tf_op | source)
XLA Modules:
  0.0 291.6 jit_solution(11246368331535473345)
XLA Ops:
  2.9 2.7 collective-permute-start.1
  5.6 1.9 collective-permute-start
  9.3 4.5 %collective-permute-start.3 = (bf16[2,1536,256]{2,1,0:T(8,128)(2,1)}, bf16[2,1536,256]{2,1,0:T(8,128)(2,1)}, u32[]{:S(2)}, u32[]{:S(2)}) collective-permute-start(bf16[2,1536,256]{2,1,0:T(8,128)(2,1)} %pad_maximum_fusion.5), channel_id=1, source_target_pairs={{8,0},{16,8},{24,16},{32,24},{40,32},{48,40},{56,48},{64,56},{72,6... | collective-permute-start | bytes 4718600 | tf_op jit(solution)/shard_map/ppermute | solution.py:25
  13.9 1.9 collective-permute-start.2
  15.8 3.2 %reshape.54 = bf16[192,8,3,128]{3,2,1,0:T(4,128)(2,1)S(1)} reshape(bf16[192,3072]{1,0:T(8,128)(2,1)} %param.8) | data formatting | bytes 2359296 | tf_op jit(solution)/shard_map/reshape | solution.py:135
  19.0 2.4 fusion.24
  22.3 6.6 %all-to-all-start = ((bf16[192,8,128]{2,0,1:T(8,128)(2,1)}), bf16[192,8,128]{2,0,1:T(8,128)(2,1)}, u32[]{:S(2)}, u32[]{:S(2)}) async-start(bf16[192,8,128]{2,0,1:T(8,128)(2,1)} %bitcast.70), calls=%async_computation | async-start | bytes 786432 | tf_op jit(solution)/shard_map/all_to_all | solution.py:137
  32.9 32.1 %all-to-all-done = bf16[192,8,128]{2,0,1:T(8,128)(2,1)} async-done(((bf16[192,8,128]{2,0,1:T(8,128)(2,1)}), bf16[192,8,128]{2,0,1:T(8,128)(2,1)}, u32[]{:S(2)}, u32[]{:S(2)}) %all-to-all-start) | async-done | bytes 393248 | tf_op jit(solution)/shard_map/all_to_all | solution.py:137
  65.0 42.3 %attention_head0.1 = (bf16[1536,128]{1,0:T(8,128)(2,1)S(1)}, bf16[1536,128]{1,0:T(8,128)(2,1)S(1)}, f32[4608,128]{1,0:T(8,128)}, f32[4608,128]{1,0:T(8,128)}) custom-call(s32[32]{0:T(128)S(1)} %reshape.53.slots_ref, s32[4]{0:T(128)S(1)} %get-tuple-element.28.counts_ref, bf16[1536,384]{1,0:T(8,128)(2,1)S(1)} %copy-done, bf16[1536,128]{1,0:T(8,128)(2,1)} %bitcast.2.do_ref, ...), custom_call_target="tpu_custom_call" | custom-call | tf_op jit(solution)/shard_map/attention_head0/pallas_call | solution.py:105
  108.8 3.5 %all-to-all-start.1 = ((bf16[8,192,128]{2,1,0:T(8,128)(2,1)}), bf16[8,192,128]{2,1,0:T(8,128)(2,1)S(1)}, u32[]{:S(2)}, u32[]{:S(2)}) async-start(bf16[8,192,128]{2,1,0:T(8,128)(2,1)} %bitcast.75), calls=%async_computation.1 | async-start | bytes 786432 | tf_op jit(solution)/shard_map/all_to_all | solution.py:165
  112.3 2.8 fusion.2
  116.3 2.0 collective-permute-start.4
  118.4 2.4 collective-permute-start.5
  121.7 6.2 %all-to-all-start.2 = ((bf16[192,8,128]{2,0,1:T(8,128)(2,1)}), bf16[192,8,128]{2,0,1:T(8,128)(2,1)}, u32[]{:S(2)}, u32[]{:S(2)}) async-start(bf16[192,8,128]{2,0,1:T(8,128)(2,1)} %bitcast.69), calls=%async_computation.2 | async-start | bytes 786432 | tf_op jit(solution)/shard_map/all_to_all | solution.py:137
  129.0 2.3 pad_maximum_fusion.3
  131.3 2.2 slice_bitcast_fusion.2
  133.5 11.6 %all-to-all-done.2 = bf16[192,8,128]{2,0,1:T(8,128)(2,1)} async-done(((bf16[192,8,128]{2,0,1:T(8,128)(2,1)}), bf16[192,8,128]{2,0,1:T(8,128)(2,1)}, u32[]{:S(2)}, u32[]{:S(2)}) %all-to-all-start.2) | async-done | bytes 393248 | tf_op jit(solution)/shard_map/all_to_all | solution.py:137
  145.1 4.1 %all-to-all-start.4 = ((bf16[192,8,128]{2,0,1:T(8,128)(2,1)}), bf16[192,8,128]{2,0,1:T(8,128)(2,1)}, u32[]{:S(2)}, u32[]{:S(2)}) async-start(bf16[192,8,128]{2,0,1:T(8,128)(2,1)} %bitcast.91), calls=%async_computation.4 | async-start | bytes 786432 | tf_op jit(solution)/shard_map/all_to_all | solution.py:137
  151.7 42.3 %attention_head1.1 = (bf16[1536,128]{1,0:T(8,128)(2,1)S(1)}, bf16[1536,128]{1,0:T(8,128)(2,1)S(1)}, f32[4608,128]{1,0:T(8,128)}, f32[4608,128]{1,0:T(8,128)}) custom-call(s32[32]{0:T(128)S(1)} %reshape.53.slots_ref, s32[4]{0:T(128)S(1)} %get-tuple-element.28.counts_ref, bf16[1536,384]{1,0:T(8,128)(2,1)S(1)} %copy-done, bf16[1536,128]{1,0:T(8,128)(2,1)} %bitcast.12.do_ref, ...), custom_call_target="tpu_custom_call" | custom-call | tf_op jit(solution)/shard_map/attention_head1/pallas_call | solution.py:105
  194.0 3.1 %fusion.1 = bf16[2,4608,128]{2,1,0:T(8,128)(2,1)S(1)} fusion(f32[1,4608,128]{2,1,0:T(8,128)} %bitcast.82, f32[1,4608,128]{2,1,0:T(8,128)} %bitcast.80), kind=kLoop, calls=%fused_computation.10 | loop fusion | flops 1179648 | bytes 7077888 | tf_op jit(solution)/shard_map/convert.6
  198.4 1.9 collective-permute-start.6
  200.3 2.4 collective-permute-start.7
  202.7 7.1 %all-to-all-start.3 = ((bf16[8,192,128]{2,1,0:T(8,128)(2,1)}), bf16[8,192,128]{2,1,0:T(8,128)(2,1)}, u32[]{:S(2)}, u32[]{:S(2)}) async-start(bf16[8,192,128]{2,1,0:T(8,128)(2,1)} %bitcast.74), calls=%async_computation.3 | async-start | bytes 786432 | tf_op jit(solution)/shard_map/all_to_all | solution.py:165
  209.8 42.4 %attention_head2.1 = (bf16[1536,128]{1,0:T(8,128)(2,1)}, bf16[1536,128]{1,0:T(8,128)(2,1)S(1)}, f32[4608,128]{1,0:T(8,128)}, f32[4608,128]{1,0:T(8,128)}) custom-call(s32[32]{0:T(128)S(1)} %reshape.53.slots_ref, s32[4]{0:T(128)S(1)} %get-tuple-element.28.counts_ref, bf16[1536,384]{1,0:T(8,128)(2,1)S(1)} %copy-done, bf16[1536,128]{1,0:T(8,128)(2,1)} %bitcast.22.do_ref, ...), custom_call_target="tpu_custom_call" | custom-call | tf_op jit(solution)/shard_map/attention_head2/pallas_call | solution.py:105
  252.3 3.0 %fusion = bf16[2,4608,128]{2,1,0:T(8,128)(2,1)S(1)} fusion(f32[1,4608,128]{2,1,0:T(8,128)} %bitcast.86, f32[1,4608,128]{2,1,0:T(8,128)} %bitcast.84), kind=kLoop, calls=%fused_computation.9 | loop fusion | flops 1179648 | bytes 7077888 | tf_op jit(solution)/shard_map/convert.4
  259.2 7.3 %all-to-all-start.5 = ((bf16[8,192,128]{2,1,0:T(8,128)(2,1)}), bf16[8,192,128]{2,1,0:T(8,128)(2,1)}, u32[]{:S(2)}, u32[]{:S(2)}) async-start(bf16[8,192,128]{2,1,0:T(8,128)(2,1)} %bitcast.25), calls=%async_computation.5 | async-start | bytes 786432 | tf_op jit(solution)/shard_map/all_to_all | solution.py:165
  266.6 1.9 collective-permute-start.8
  268.6 2.4 collective-permute-start.9
  273.4 2.7 all-to-all-done.5
  277.6 2.8 copy.36
  280.3 4.1 %reshape.55 = bf16[192,3072]{1,0:T(8,128)(2,1)} reshape(bf16[192,8,3,128]{3,2,1,0:T(4,128)(2,1)} %copy.36) | data formatting | bytes 2359296 | tf_op jit(solution)/shard_map/reshape | solution.py:171
  284.5 2.0 fusion.8
  (94 shorter events, 30.3 us)
Async XLA Ops:
  0.6 6.9 %copy-start.22 = (bf16[1536,384]{1,0:T(8,128)(2,1)S(1)}, bf16[1536,384]{1,0:T(8,128)(2,1)}, u32[]{:S(2)}) copy-start(bf16[1536,384]{1,0:T(8,128)(2,1)} %param.7) | copy-start | bytes 3538948
  0.6 6.9 %copy-start.23 = (bf16[1536,384]{1,0:T(8,128)(2,1)S(1)}, bf16[1536,384]{1,0:T(8,128)(2,1)}, u32[]{:S(2)}) copy-start(bf16[1536,384]{1,0:T(8,128)(2,1)} %param.6) | copy-start | bytes 3538948
  2.9 28.3 %collective-permute-start.1 = (bf16[2,1536,128]{2,1,0:T(8,128)(2,1)}, bf16[2,1536,128]{2,1,0:T(8,128)(2,1)}, u32[]{:S(2)}, u32[]{:S(2)}) collective-permute-start(bf16[2,1536,128]{2,1,0:T(8,128)(2,1)} %pad_maximum_fusion.10), channel_id=1, source_target_pairs={{8,0},{16,8},{24,16},{32,24},{40,32},{48,40},{56,48},{64,56},{72,6... | collective-permute-start | bytes 2359304 | tf_op jit(solution)/shard_map/ppermute | solution.py:25
  5.6 25.6 %collective-permute-start = (bf16[2,1536,128]{2,1,0:T(8,128)(2,1)}, bf16[2,1536,128]{2,1,0:T(8,128)(2,1)}, u32[]{:S(2)}, u32[]{:S(2)}) collective-permute-start(bf16[2,1536,128]{2,1,0:T(8,128)(2,1)} %pad_maximum_fusion.10), channel_id=1, source_target_pairs={{0,8},{8,16},{16,24},{24,32},{32,40},{40,48},{48,56},{56,64},{64,7... | collective-permute-start | bytes 2359304 | tf_op jit(solution)/shard_map/ppermute | solution.py:24
  9.3 119.6 %collective-permute-start.3 = (bf16[2,1536,256]{2,1,0:T(8,128)(2,1)}, bf16[2,1536,256]{2,1,0:T(8,128)(2,1)}, u32[]{:S(2)}, u32[]{:S(2)}) collective-permute-start(bf16[2,1536,256]{2,1,0:T(8,128)(2,1)} %pad_maximum_fusion.5), channel_id=1, source_target_pairs={{8,0},{16,8},{24,16},{32,24},{40,32},{48,40},{56,48},{64,56},{72,6... | collective-permute-start | bytes 4718600 | tf_op jit(solution)/shard_map/ppermute | solution.py:25
  13.9 115.1 %collective-permute-start.2 = (bf16[2,1536,256]{2,1,0:T(8,128)(2,1)}, bf16[2,1536,256]{2,1,0:T(8,128)(2,1)}, u32[]{:S(2)}, u32[]{:S(2)}) collective-permute-start(bf16[2,1536,256]{2,1,0:T(8,128)(2,1)} %pad_maximum_fusion.5), channel_id=1, source_target_pairs={{0,8},{8,16},{16,24},{24,32},{32,40},{40,48},{48,56},{56,64},{64,7... | collective-permute-start | bytes 4718600 | tf_op jit(solution)/shard_map/ppermute | solution.py:24
  21.4 7.5 %copy-start.24 = (s32[64,8]{0,1:T(8,128)S(1)}, s32[64,8]{0,1:T(8,128)}, u32[]{:S(2)}) copy-start(s32[64,8]{0,1:T(8,128)} %param.9) | copy-start | bytes 6148
  21.4 7.9 %copy-start.20 = (bf16[192,8,1,128]{3,2,1,0:T(2,128)(2,1)S(1)}, bf16[192,8,1,128]{3,2,1,0:T(2,128)(2,1)}, u32[]{:S(2)}) copy-start(bf16[192,8,1,128]{3,2,1,0:T(2,128)(2,1)} %get-tuple-element.43) | copy-start | bytes 1179652
  22.3 42.7 %all-to-all-start = ((bf16[192,8,128]{2,0,1:T(8,128)(2,1)}), bf16[192,8,128]{2,0,1:T(8,128)(2,1)}, u32[]{:S(2)}, u32[]{:S(2)}) async-start(bf16[192,8,128]{2,0,1:T(8,128)(2,1)} %bitcast.70), calls=%async_computation | async-start | bytes 786432 | tf_op jit(solution)/shard_map/all_to_all | solution.py:137
  32.7 32.3 %copy-start = (bf16[1536,384]{1,0:T(8,128)(2,1)S(1)}, bf16[1536,384]{1,0:T(8,128)(2,1)}, u32[]{:S(2)}) copy-start(bf16[1536,384]{1,0:T(8,128)(2,1)} %q_ref.5) | copy-start | bytes 3538948
  108.8 12.9 %all-to-all-start.1 = ((bf16[8,192,128]{2,1,0:T(8,128)(2,1)}), bf16[8,192,128]{2,1,0:T(8,128)(2,1)S(1)}, u32[]{:S(2)}, u32[]{:S(2)}) async-start(bf16[8,192,128]{2,1,0:T(8,128)(2,1)} %bitcast.75), calls=%async_computation.1 | async-start | bytes 786432 | tf_op jit(solution)/shard_map/all_to_all | solution.py:165
  116.3 12.6 %copy-start.17 = (bf16[1,1536,256]{2,1,0:T(8,128)(2,1)S(1)}, bf16[1,1536,256]{2,1,0:T(8,128)(2,1)}, u32[]{:S(2)}) copy-start(bf16[1,1536,256]{2,1,0:T(8,128)(2,1)} %copy-done.16) | copy-start | bytes 2359300
  116.3 12.6 %copy-start.19 = (bf16[1,1536,256]{2,1,0:T(8,128)(2,1)S(1)}, bf16[1,1536,256]{2,1,0:T(8,128)(2,1)}, u32[]{:S(2)}) copy-start(bf16[1,1536,256]{2,1,0:T(8,128)(2,1)} %copy-done.18) | copy-start | bytes 2359300
  116.3 140.2 %collective-permute-start.4 = (bf16[2,1536,128]{2,1,0:T(8,128)(2,1)}, bf16[2,1536,128]{2,1,0:T(8,128)(2,1)}, u32[]{:S(2)}, u32[]{:S(2)}) collective-permute-start(bf16[2,1536,128]{2,1,0:T(8,128)(2,1)} %get-tuple-element.34), channel_id=1, source_target_pairs={{8,0},{16,8},{24,16},{32,24},{40,32},{48,40},{56,48},{64,56},{72,6... | collective-permute-start | bytes 2359304 | tf_op jit(solution)/shard_map/ppermute | solution.py:32
  118.4 138.1 %collective-permute-start.5 = (bf16[2,1536,128]{2,1,0:T(8,128)(2,1)}, bf16[2,1536,128]{2,1,0:T(8,128)(2,1)}, u32[]{:S(2)}, u32[]{:S(2)}) collective-permute-start(bf16[2,1536,128]{2,1,0:T(8,128)(2,1)} %get-tuple-element.35), channel_id=1, source_target_pairs={{0,8},{8,16},{16,24},{24,32},{32,40},{40,48},{48,56},{56,64},{64,7... | collective-permute-start | bytes 2359304 | tf_op jit(solution)/shard_map/ppermute | solution.py:32
  121.7 23.4 %all-to-all-start.2 = ((bf16[192,8,128]{2,0,1:T(8,128)(2,1)}), bf16[192,8,128]{2,0,1:T(8,128)(2,1)}, u32[]{:S(2)}, u32[]{:S(2)}) async-start(bf16[192,8,128]{2,0,1:T(8,128)(2,1)} %bitcast.69), calls=%async_computation.2 | async-start | bytes 786432 | tf_op jit(solution)/shard_map/all_to_all | solution.py:137
  145.1 57.6 %all-to-all-start.4 = ((bf16[192,8,128]{2,0,1:T(8,128)(2,1)}), bf16[192,8,128]{2,0,1:T(8,128)(2,1)}, u32[]{:S(2)}, u32[]{:S(2)}) async-start(bf16[192,8,128]{2,0,1:T(8,128)(2,1)} %bitcast.91), calls=%async_computation.4 | async-start | bytes 786432 | tf_op jit(solution)/shard_map/all_to_all | solution.py:137
  194.0 3.1 %copy-start.5 = (bf16[1536,128]{1,0:T(8,128)(2,1)}, bf16[1536,128]{1,0:T(8,128)(2,1)S(1)}, u32[]{:S(2)}) copy-start(bf16[1536,128]{1,0:T(8,128)(2,1)S(1)} %get-tuple-element.20) | copy-start | bytes 1179652
  194.0 3.1 %copy-start.9 = (bf16[1536,128]{1,0:T(8,128)(2,1)}, bf16[1536,128]{1,0:T(8,128)(2,1)S(1)}, u32[]{:S(2)}) copy-start(bf16[1536,128]{1,0:T(8,128)(2,1)S(1)} %get-tuple-element.17) | copy-start | bytes 1179652
  198.4 86.1 %collective-permute-start.6 = (bf16[2,1536,128]{2,1,0:T(8,128)(2,1)}, bf16[2,1536,128]{2,1,0:T(8,128)(2,1)}, u32[]{:S(2)}, u32[]{:S(2)}) collective-permute-start(bf16[2,1536,128]{2,1,0:T(8,128)(2,1)} %get-tuple-element.36), channel_id=1, source_target_pairs={{8,0},{16,8},{24,16},{32,24},{40,32},{48,40},{56,48},{64,56},{72,6... | collective-permute-start | bytes 2359304 | tf_op jit(solution)/shard_map/ppermute | solution.py:32
  200.3 84.2 %collective-permute-start.7 = (bf16[2,1536,128]{2,1,0:T(8,128)(2,1)}, bf16[2,1536,128]{2,1,0:T(8,128)(2,1)}, u32[]{:S(2)}, u32[]{:S(2)}) collective-permute-start(bf16[2,1536,128]{2,1,0:T(8,128)(2,1)} %get-tuple-element.37), channel_id=1, source_target_pairs={{0,8},{8,16},{16,24},{24,32},{32,40},{40,48},{48,56},{56,64},{64,7... | collective-permute-start | bytes 2359304 | tf_op jit(solution)/shard_map/ppermute | solution.py:32
  202.7 56.5 %all-to-all-start.3 = ((bf16[8,192,128]{2,1,0:T(8,128)(2,1)}), bf16[8,192,128]{2,1,0:T(8,128)(2,1)}, u32[]{:S(2)}, u32[]{:S(2)}) async-start(bf16[8,192,128]{2,1,0:T(8,128)(2,1)} %bitcast.74), calls=%async_computation.3 | async-start | bytes 786432 | tf_op jit(solution)/shard_map/all_to_all | solution.py:165
  252.3 4.3 %copy-start.12 = (f32[4608,128]{1,0:T(8,128)S(1)}, f32[4608,128]{1,0:T(8,128)}, u32[]{:S(2)}) copy-start(f32[4608,128]{1,0:T(8,128)} %get-tuple-element.23) | copy-start | bytes 7077892
  259.1 11.9 %copy-start.4 = (bf16[1536,128]{1,0:T(8,128)(2,1)S(1)}, bf16[1536,128]{1,0:T(8,128)(2,1)}, u32[]{:S(2)}) copy-start(bf16[1536,128]{1,0:T(8,128)(2,1)} %copy-done.3) | copy-start | bytes 1179652
  259.1 11.9 %copy-start.6 = (bf16[1536,128]{1,0:T(8,128)(2,1)S(1)}, bf16[1536,128]{1,0:T(8,128)(2,1)}, u32[]{:S(2)}) copy-start(bf16[1536,128]{1,0:T(8,128)(2,1)} %copy-done.5) | copy-start | bytes 1179652
  259.1 11.9 %copy-start.8 = (bf16[1536,128]{1,0:T(8,128)(2,1)S(1)}, bf16[1536,128]{1,0:T(8,128)(2,1)}, u32[]{:S(2)}) copy-start(bf16[1536,128]{1,0:T(8,128)(2,1)} %copy-done.7) | copy-start | bytes 1179652
  259.2 16.9 %all-to-all-start.5 = ((bf16[8,192,128]{2,1,0:T(8,128)(2,1)}), bf16[8,192,128]{2,1,0:T(8,128)(2,1)}, u32[]{:S(2)}, u32[]{:S(2)}) async-start(bf16[8,192,128]{2,1,0:T(8,128)(2,1)} %bitcast.25), calls=%async_computation.5 | async-start | bytes 786432 | tf_op jit(solution)/shard_map/all_to_all | solution.py:165
  266.6 19.9 %collective-permute-start.8 = (bf16[2,1536,128]{2,1,0:T(8,128)(2,1)}, bf16[2,1536,128]{2,1,0:T(8,128)(2,1)}, u32[]{:S(2)}, u32[]{:S(2)}) collective-permute-start(bf16[2,1536,128]{2,1,0:T(8,128)(2,1)} %get-tuple-element.38), channel_id=1, source_target_pairs={{8,0},{16,8},{24,16},{32,24},{40,32},{48,40},{56,48},{64,56},{72,6... | collective-permute-start | bytes 2359304 | tf_op jit(solution)/shard_map/ppermute | solution.py:32
  268.6 18.0 %collective-permute-start.9 = (bf16[2,1536,128]{2,1,0:T(8,128)(2,1)}, bf16[2,1536,128]{2,1,0:T(8,128)(2,1)}, u32[]{:S(2)}, u32[]{:S(2)}) collective-permute-start(bf16[2,1536,128]{2,1,0:T(8,128)(2,1)} %get-tuple-element.39), channel_id=1, source_target_pairs={{0,8},{8,16},{16,24},{24,32},{32,40},{40,48},{48,56},{56,64},{64,7... | collective-permute-start | bytes 2359304 | tf_op jit(solution)/shard_map/ppermute | solution.py:32
  271.0 6.4 %copy-start.21 = (bf16[8,192,128]{2,0,1:T(8,128)(2,1)S(1)}, bf16[8,192,128]{2,0,1:T(8,128)(2,1)}, u32[]{:S(2)}) copy-start(bf16[8,192,128]{2,0,1:T(8,128)(2,1)} %copy.51) | copy-start | bytes 1179652
  280.3 4.1 %copy-start.13 = (f32[4608,128]{1,0:T(8,128)S(1)}, f32[4608,128]{1,0:T(8,128)}, u32[]{:S(2)}) copy-start(f32[4608,128]{1,0:T(8,128)} %get-tuple-element.24) | copy-start | bytes 7077892
  284.5 3.1 %copy-start.15 = (f32[4608,128]{1,0:T(8,128)S(1)}, f32[4608,128]{1,0:T(8,128)}, u32[]{:S(2)}) copy-start(f32[4608,128]{1,0:T(8,128)} %get-tuple-element.27) | copy-start | bytes 7077892
  (9 other events, 14.8 us)
